TPU v7x, 128 devices: a whole 4x4x4 slice. The times are simulated.
128 devices in a mesh: half: 2 (over core), row: 8 (over z_hi, x), col: 8 (over y, z_lo).
Axes of the slice: x: 4, y: 4, z: 4 (z_hi: 2, z_lo: 2; z = z_hi * 2 + z_lo), core: 2. Of those that a mesh axis runs over, the one named last changes fastest.
Arguments:
- child_diag: float32 [2, 512, 512], P('half'), as said below
- child_panel: float32 [2, 16, 8, 128, 512], P('half', None, 'row'), may hold values from -18 to 18
- child_window: float32 [2, 16, 8, 128, 8, 8, 128], P('half', None, 'row', None, None, 'col'), may hold values from -6 to 6
- parent_diag: float32 [512, 512], replicated
- parent_lead_panel: float32 [24, 8, 2, 8, 8, 512], P(None, 'row', 'half', 'col'), may hold values from -24 to 24
- index_maps: int32 [2, 128], replicated, may hold values from 0 to 191, as said below
Outputs:
- parent_front: float32 [24, 8, 128, 4, 2, 8, 128], P(None, 'row', None, None, 'half', 'col')
- parent_factor: float32 [24, 8, 2, 8, 8, 512], P(None, 'row', 'half', 'col')
- parent_pivot: float32 [512, 512], replicated
Inputs may be any that keep to these rules, and one draw needn't show every extreme that they name: child_diag and parent_diag are symmetric and positive definite. For each child k and each group a, the entries index_maps[k, a * 16 + u] with 0 <= u < 16 equal q * 16 + ((u + s) mod 16) for a group target q and a turn s fixed within the group; groups a < 4 have q = a, later groups have distinct q that rise with a; over the 8 groups of a child the turns s, taken modulo 8, are all different; for each child some group a < 4 has a turn divisible by 8, and another group a < 4 has a turn that leaves 1 modulo 8.
All inputs are finite; a program needn't handle non-finite values.
Results may differ from a plain program's by a relative error of at most 0.0001.
Values sent between devices are 32-bit elements; how exact they have to be, the bound alone decides.
No kernel may reach another device: no remote copies, remote signals or barrier semaphores. Data moves between devices by JAX's collectives and lax.ppermute only.
A program may use at most 192 MiB of HBM per device.

v0:
```python
import jax
import jax.numpy as jnp
from jax import lax
from jax.sharding import PartitionSpec as P

BLOCK_EXTENT = 128
PB = 4
SB = 128
RB = 192
WB = 64


def from_root(shard, axis, root):
    mine = lax.axis_index(axis) == root
    return lax.psum(jnp.where(mine, shard, jnp.zeros_like(shard)), axis)


def pick_ranked(owners, values, wanted, slot_count, missing):
    matches = owners[..., None, :] == wanted[:, None]
    ranking = jnp.cumsum(matches.astype(jnp.int32), axis=-1) - 1
    slot_ids = jnp.arange(slot_count, dtype=jnp.int32)
    chosen = matches[..., None, :] & (ranking[..., None, :] == slot_ids[:, None])
    present = jnp.any(chosen, axis=-1)
    picked = jnp.sum(jnp.where(chosen, values[..., None, None, :], 0), axis=-1)
    return jnp.where(present, picked, missing)


def per_device(child_diag, child_panel, child_window, parent_diag, parent_lead_panel, index_maps):
    highest = lax.Precision.HIGHEST
    row_size = lax.axis_size("row")
    half_id = lax.axis_index("half")
    row_id = lax.axis_index("row")
    col_id = lax.axis_index("col")
    panel_width = PB * BLOCK_EXTENT
    group_size = 2 * row_size
    row_local = SB // row_size
    col_local = WB // row_size
    parent_row_blocks = RB // row_size
    parent_cols = WB // group_size
    per_row = 2 * (SB // group_size) // row_size
    per_col = (WB // group_size + row_size - 1) // row_size
    pivot_lower_factor = jnp.linalg.cholesky(parent_diag)
    own_rows = parent_lead_panel.reshape(-1, panel_width)
    solved = jax.scipy.linalg.solve_triangular(pivot_lower_factor, own_rows.T, lower=True).T
    parent_factor = solved.reshape(parent_lead_panel.shape)
    sub_rows = parent_lead_panel.shape[4]
    gathered = lax.all_gather(
        solved.reshape(parent_row_blocks, sub_rows, panel_width),
        ("half", "col"),
        axis=1,
        tiled=True,
    )
    paired = gathered[: 2 * parent_cols].reshape(parent_cols, 2, BLOCK_EXTENT, panel_width)
    offered = lax.dynamic_index_in_dim(paired, half_id, axis=1, keepdims=False)
    column_factor = from_root(offered, "row", col_id)
    child_low = jnp.linalg.cholesky(child_diag[0])
    child_rows = child_panel.reshape(-1, panel_width)
    child_factor = jax.scipy.linalg.solve_triangular(child_low, child_rows.T, lower=True).T
    leading = child_factor[: col_local * BLOCK_EXTENT]
    everyone = lax.all_gather(leading[None], "row", axis=0, tiled=True)
    child_columns = lax.dynamic_index_in_dim(everyone, col_id, axis=0, keepdims=False)
    schur_part = child_window.reshape(row_local * BLOCK_EXTENT, col_local * BLOCK_EXTENT) - jnp.dot(
        child_factor, child_columns.T, precision=highest
    )
    schur_blocks = schur_part.reshape(row_local, BLOCK_EXTENT, col_local, BLOCK_EXTENT)
    child_map = lax.dynamic_index_in_dim(index_maps, half_id, axis=0, keepdims=False)
    my_rows = lax.dynamic_index_in_dim(
        child_map.reshape(row_local, row_size), row_id, axis=1, keepdims=False
    )
    my_cols = lax.dynamic_index_in_dim(
        child_map[:WB].reshape(col_local, row_size), col_id, axis=1, keepdims=False
    )
    local_rows = jnp.arange(row_local, dtype=jnp.int32)
    local_cols = jnp.arange(col_local, dtype=jnp.int32)
    send_rows = pick_ranked(
        my_rows % row_size, local_rows, jnp.arange(row_size, dtype=jnp.int32), per_row, row_local
    )
    send_cols = pick_ranked(
        my_cols % group_size,
        local_cols,
        jnp.arange(group_size, dtype=jnp.int32),
        per_col,
        col_local,
    )
    all_rows = index_maps.reshape(2, row_local, row_size).transpose(0, 2, 1)
    row_target = pick_ranked(
        all_rows % row_size, all_rows // row_size, row_id[None], per_row, parent_row_blocks
    )[:, :, 0, :]
    all_cols = index_maps[:, :WB].reshape(2, col_local, row_size).transpose(0, 2, 1)
    col_target = pick_ranked(
        all_cols % group_size,
        all_cols // group_size,
        (half_id * row_size + col_id)[None],
        per_col,
        parent_cols,
    )[:, :, 0, :]
    assembled_front = jnp.zeros(
        (parent_row_blocks, BLOCK_EXTENT, parent_cols, BLOCK_EXTENT), jnp.float32
    )
    row_index = send_rows[None, :, None, :, None]
    col_index = send_cols.reshape(2, row_size, per_col)[:, None, :, None, :]
    outgoing = schur_blocks.at[row_index, :, col_index, :].get(mode="fill", fill_value=0.0)
    arrived = lax.all_to_all(
        outgoing.reshape(-1, per_row * per_col, BLOCK_EXTENT, BLOCK_EXTENT),
        ("half", "row", "col"),
        split_axis=0,
        concat_axis=0,
        tiled=True,
    )
    arrived = arrived.reshape(2, row_size, row_size, per_row, per_col, BLOCK_EXTENT, BLOCK_EXTENT)
    target_rows = row_target[:, :, None, :, None]
    target_cols = col_target[:, None, :, None, :]
    assembled_front = assembled_front.at[target_rows, :, target_cols, :].add(arrived, mode="drop")
    flat_front = assembled_front.reshape(
        parent_row_blocks * BLOCK_EXTENT, parent_cols * BLOCK_EXTENT
    )
    updated = flat_front - jnp.dot(
        gathered.reshape(-1, panel_width),
        column_factor.reshape(-1, panel_width).T,
        precision=highest,
    )
    return (
        updated.reshape(parent_row_blocks, 1, BLOCK_EXTENT, parent_cols, 1, 1, BLOCK_EXTENT),
        parent_factor,
        pivot_lower_factor,
    )


def solution(mesh):
    in_specs = (
        P("half", None, None),
        P("half", None, "row", None, None),
        P("half", None, "row", None, None, "col", None),
        P(),
        P(None, "row", "half", "col", None, None),
        P(),
    )
    out_specs = (
        P(None, "row", None, None, "half", "col", None),
        P(None, "row", "half", "col", None, None),
        P(),
    )
    return jax.shard_map(
        per_device, mesh=mesh, in_specs=in_specs, out_specs=out_specs, check_vma=False
    )
```

profile of v0, /device:TPU:0, one launch (start us, length us, event | category | flops | bytes accessed | tf_op | source)
XLA Modules:
  0.0 819.9 jit_solution(16038382859682363218)
XLA Ops:
  14.1 11.7 %cholesky.286 = f32[128,128]{1,0:T(8,128)S(1)} custom-call(f32[128,128]{1,0:T(8,128)S(1)} %cholesky.426), custom_call_target="Cholesky" | custom-call | tf_op jit(solution)/shard_map/jit(cholesky)/cholesky | solution.py:56
  26.0 9.8 %custom-call.37 = f32[1,128,128]{1,2,0:T(8,128)S(1)} custom-call(f32[1,128,128]{2,1,0:T(8,128)S(1)} %get-tuple-element.91), custom_call_target="InvertDiagBlocksLowerTriangular" | custom-call | tf_op jit(solution)/shard_map/jit(cholesky)/cholesky | solution.py:56
  36.5 11.7 %cholesky.305 = f32[128,128]{1,0:T(8,128)S(1)} custom-call(f32[128,128]{1,0:T(8,128)S(1)} %cholesky.430), custom_call_target="Cholesky" | custom-call | tf_op jit(solution)/shard_map/jit(cholesky)/cholesky | solution.py:56
  48.2 10.2 %custom-call.38 = f32[1,128,128]{1,2,0:T(8,128)S(1)} custom-call(f32[1,128,128]{2,1,0:T(8,128)S(1)} %get-tuple-element.88), custom_call_target="InvertDiagBlocksLowerTriangular" | custom-call | tf_op jit(solution)/shard_map/jit(cholesky)/cholesky | solution.py:56
  59.1 11.7 %cholesky.326 = f32[128,128]{1,0:T(8,128)S(1)} custom-call(f32[128,128]{1,0:T(8,128)S(1)} %cholesky.435), custom_call_target="Cholesky" | custom-call | tf_op jit(solution)/shard_map/jit(cholesky)/cholesky | solution.py:56
  70.9 9.8 %custom-call.39 = f32[1,128,128]{1,2,0:T(8,128)S(1)} custom-call(f32[1,128,128]{2,1,0:T(8,128)S(1)} %get-tuple-element.85), custom_call_target="InvertDiagBlocksLowerTriangular" | custom-call | tf_op jit(solution)/shard_map/jit(cholesky)/cholesky | solution.py:56
  81.3 11.7 %cholesky.343 = f32[128,128]{1,0:T(8,128)S(1)} custom-call(f32[128,128]{1,0:T(8,128)S(1)} %convolution_subtract_fusion.10), custom_call_target="Cholesky" | custom-call | tf_op jit(solution)/shard_map/jit(cholesky)/cholesky | solution.py:56
  106.4 39.3 %custom-call.28 = f32[4,128,128]{1,2,0:T(8,128)S(1)} custom-call(f32[4,128,128]{2,1,0:T(8,128)S(1)} %get-tuple-element.11), custom_call_target="InvertDiagBlocksLowerTriangular" | custom-call | tf_op jit(solution)/shard_map/jit(_solve_triangular)/triangular_solve | solution.py:58
  169.6 11.9 %cholesky.358 = f32[128,128]{1,0:T(8,128)S(1)} custom-call(f32[128,128]{1,0:T(8,128)S(1)} %cholesky.439), custom_call_target="Cholesky" | custom-call | tf_op jit(solution)/shard_map/jit(cholesky)/cholesky | solution.py:42
  195.7 11.7 %cholesky.377 = f32[128,128]{1,0:T(8,128)S(1)} custom-call(f32[128,128]{1,0:T(8,128)S(1)} %cholesky.443), custom_call_target="Cholesky" | custom-call | tf_op jit(solution)/shard_map/jit(cholesky)/cholesky | solution.py:42
  208.1 9.8 %custom-call.41 = f32[1,128,128]{1,2,0:T(8,128)S(1)} custom-call(f32[1,128,128]{2,1,0:T(8,128)S(1)} %get-tuple-element.78), custom_call_target="InvertDiagBlocksLowerTriangular" | custom-call | tf_op jit(solution)/shard_map/jit(cholesky)/cholesky | solution.py:42
  220.2 12.1 %cholesky.398 = f32[128,128]{1,0:T(8,128)S(1)} custom-call(f32[128,128]{1,0:T(8,128)S(1)} %cholesky.448), custom_call_target="Cholesky" | custom-call | tf_op jit(solution)/shard_map/jit(cholesky)/cholesky | solution.py:42
  245.1 11.7 %cholesky.415 = f32[128,128]{1,0:T(8,128)S(1)} custom-call(f32[128,128]{1,0:T(8,128)S(1)} %convolution_subtract_fusion.9), custom_call_target="Cholesky" | custom-call | tf_op jit(solution)/shard_map/jit(cholesky)/cholesky | solution.py:42
  260.6 89.0 %all-gather.6.cloned.1.call-done = f32[8192,512]{0,1:T(8,128)} async-done(((f32[1024,512]{0,1:T(8,128)}), f32[8192,512]{0,1:T(8,128)}) %all-gather.6.cloned.1.call-update) | async-done | bytes 16777232 | tf_op jit(solution)/shard_map/all_gather | solution.py:60
  349.5 21.3 %copy.78 = f32[64,8,8,1024]{3,2,1,0:T(8,128)} copy(f32[64,8,8,1024]{3,1,2,0:T(8,128)} %bitcast.224) | data formatting | bytes 33554432
  380.3 20.5 %fusion = f32[256,8,8,128]{3,1,2,0:T(8,128)S(1)} fusion(f32[256,8,8,128]{3,2,1,0:T(8,128)} %bitcast.231, f32[128,2048]{1,0:T(8,128)} %copy-done.1, f32[128,2048]{1,0:T(8,128)S(1)} %fusion.56, f32[128,2048]{1,0:T(8,128)S(1)} %fusion.58, f32[128,2048]{1,0:T(8,128)S(1)} %fusion.16, f32[1,1024,512]{1,0,2:T(1,128)} %constant_dynamic-slice_fusion.2), kind=kOutput, calls=%fused_computation.7 | convolution fusion | flops 12890144768 | bytes 23068672 | tf_op jit(solution)/shard_map/dot_general | solution.py:62
  407.6 16.0 %gather_fusion = f32[256,128,128]{2,1,0:T(8,128)} fusion(f32[16,128,8,128]{3,1,2,0:T(8,128)} %copy.67, s32[256]{0:T(256)S(1)} %reshape.575), kind=kCustom, calls=%fused_computation | custom fusion | bytes 33556480 | tf_op jit(solution)/shard_map/gather | solution.py:102
  423.6 11.4 %broadcast_select_fusion = f32[128,2,128,128]{3,2,1,0:T(8,128)} fusion(f32[128,2,128,128]{3,2,1,0:T(8,128)} %bitcast.220, pred[128,2]{1,0:T(8,128)(4,1)S(1)} %bitcast.239), kind=kLoop, calls=%fused_computation.8 | loop fusion | flops 4194304 | bytes 33554688 | tf_op jit(solution)/shard_map/select_n | solution.py:102
  453.0 39.3 %custom-call.29 = f32[4,128,128]{1,2,0:T(8,128)S(1)} custom-call(f32[4,128,128]{2,1,0:T(8,128)S(1)} %get-tuple-element.19), custom_call_target="InvertDiagBlocksLowerTriangular" | custom-call | tf_op jit(solution)/shard_map/jit(_solve_triangular)/triangular_solve | solution.py:44
  495.5 205.3 %all-gather.4.cloned.1.call-done = f32[24,128,512]{2,1,0:T(8,128)} async-done(((f32[24,8,512]{2,1,0:T(8,128)}), f32[24,128,512]{2,1,0:T(8,128)}) %all-gather.4.cloned.1.call-update) | async-done | bytes 6291472 | tf_op jit(solution)/shard_map/all_gather | solution.py:47
  708.1 51.8 %scatter_fusion = f32[24,128,4,128]{3,1,2,0:T(8,128)} fusion(f32[24,128,4,128]{3,1,2,0:T(8,128)} %broadcast_in_dim.109, s32[256]{0:T(256)S(1)} %reshape.583, f32[256,128,128]{2,1,0:T(8,128)} %bitcast.23), kind=kCustom, calls=%fused_computation.1 | custom fusion | flops 4194304 | bytes 50333696 | tf_op jit(solution)/shard_map/scatter-add | solution.py:113
  759.9 10.5 %copy.68 = f32[24,128,4,128]{3,2,1,0:T(4,128)} copy(f32[24,128,4,128]{3,1,2,0:T(8,128)} %scatter_fusion) | data formatting | bytes 12582912 | tf_op jit(solution)/shard_map/scatter-add | solution.py:113
  770.4 18.2 %all-reduce.3.cloned.1.call-done = f32[512,512]{1,0:T(8,128)} async-done(((f32[512,512]{1,0:T(8,128)}), f32[512,512]{1,0:T(8,128)}) %all-reduce.3.cloned.1.call-update) | async-done | bytes 1048592 | tf_op jit(solution)/shard_map/psum | solution.py:15
  788.6 16.1 %bitcast_subtract_fusion.1 = f32[3072,512]{1,0:T(8,128)} fusion(f32[384,8,4,128]{3,2,1,0:T(4,128)} %bitcast.222, f32[3072,512]{1,0:T(8,128)} %bitcast.229, f32[512,512]{1,0:T(8,128)} %all-reduce.3.cloned.1.call-done), kind=kOutput, calls=%fused_computation.9 | convolution fusion | flops 9665249280 | bytes 19922944 | tf_op jit(solution)/shard_map/dot_general | solution.py:117
  (173 shorter events, 142.2 us)
Async XLA Ops:
  8.0 341.5 %all-gather.6.cloned.1.call-start = ((), (), s32[]{:S(2)}) async-start(), calls=%async_computation.3 | async-start | bytes 18874368 | tf_op jit(solution)/shard_map/all_gather | solution.py:60
  8.1 5.4 copy-start.3
  106.4 45.1 %copy-start.4 = (f32[512,512]{1,0:T(8,128)}, f32[512,512]{1,0:T(8,128)S(1)}, u32[]{:S(2)}) copy-start(f32[512,512]{1,0:T(8,128)S(1)} %get-tuple-element.206) | copy-start | bytes 3145732
  145.7 5.7 copy-start
  157.9 1.0 copy-start.1
  159.1 2.1 copy-start.7
  159.2 4.8 copy-start.8
  168.6 1.0 copy-start.5
  435.0 8.2 %copy-start.2 = (f32[512,512]{1,0:T(8,128)S(1)}, f32[512,512]{1,0:T(8,128)}, u32[]{:S(2)}) copy-start(f32[512,512]{1,0:T(8,128)} %get-tuple-element.73) | copy-start | bytes 3145732
  435.0 269.6 %all-to-all-start = ((f32[128,2,128,128]{3,2,1,0:T(8,128)}), f32[128,2,128,128]{3,2,1,0:T(8,128)}, u32[]{:S(2)}, u32[]{:S(2)}) async-start(f32[128,2,128,128]{3,2,1,0:T(8,128)} %broadcast_select_fusion), calls=%async_computation | async-start | bytes 33554432 | tf_op jit(solution)/shard_map/all_to_all | solution.py:103
  441.9 50.4 %copy-start.6 = (f32[24,1,1,1,8,512]{5,4,3,2,1,0:T(8,128)S(1)}, f32[24,1,1,1,8,512]{5,4,3,2,1,0:T(8,128)}, u32[]{:S(2)}) copy-start(f32[24,1,1,1,8,512]{5,4,3,2,1,0:T(8,128)} %param.11) | copy-start | bytes 1179652
  441.9 258.9 %all-gather.4.cloned.1.call-start = ((), (), s32[]{:S(2)}) async-start(), calls=%async_computation.1 | async-start | bytes 6684672 | tf_op jit(solution)/shard_map/all_gather | solution.py:47
  495.3 293.3 %all-reduce.3.cloned.1.call-start = ((), (), s32[]{:S(2)}) async-start(), calls=%async_computation.2 | async-start | bytes 2097152 | tf_op jit(solution)/shard_map/psum | solution.py:15
  700.8 1.6 slice-start
Sparse Core Ops, SparseCore 0:
  160.9 188.6 all-gather.5
  703.6 84.9 all-reduce.2
Sparse Core Ops, SparseCore 1:
  495.4 205.4 all-gather.3
where the time goes:
time: 830 us; the launch traced here: 820 us
  waiting for transfers between devices  313 us (38%)
  other arithmetic  309 us (37%)
  local copies, waits for them, and re-layouts  109 us (13%)
  matrix products  60.3 us (7%)
  between operations  21.3 us (3%)
    all_gather x1, waiting for transfers between devices, per_device(): lax.all_gather(solved.reshape(parent_row_blocks, sub_rows, panel_width),...  205 us
    all_gather x1, waiting for transfers between devices, per_device(): everyone = lax.all_gather(leading[None], 'row', axis=0, tiled=True)  89 us
    another operation x14, other arithmetic, per_device(): pivot_lower_factor = jnp.linalg.cholesky(parent_diag)  80.7 us
    another operation x14, other arithmetic, per_device(): child_low = jnp.linalg.cholesky(child_diag[0])  78.9 us
    scatter-add x1, other arithmetic, per_device(): assembled_front.at[target_rows, :, target_cols, :].add(arrived, mode='drop')  51.8 us
    another operation x2, other arithmetic, per_device(): jax.scipy.linalg.solve_triangular(pivot_lower_factor, own_rows.T, lower=T...  40.6 us
    another operation x3, other arithmetic, per_device(): jax.scipy.linalg.solve_triangular(child_low, child_rows.T, lower=True)  39.4 us
    unnamed x24, local copies, waits for them, and re-layouts  28.3 us
  transfers between devices with their start and end apart: 4, of which 3 were waited for; matrix products, arithmetic and copies ran while one was open for 26% of the time, Pallas kernels for 0%

commit v1 on v0

--- a/solution.py
+++ b/solution.py
@@ -57,7 +57,16 @@
     child_rows = child_panel.reshape(-1, panel_width)
     child_factor = jax.scipy.linalg.solve_triangular(child_low, child_rows.T, lower=True).T
     leading = child_factor[: col_local * BLOCK_EXTENT]
-    everyone = lax.all_gather(leading[None], "row", axis=0, tiled=True)
+    array_here = leading[None]
+    everyone = jnp.concatenate(
+        lax.all_to_all(
+            jnp.stack(lax.axis_size("row") * [array_here]),
+            axis_name="row",
+            split_axis=0,
+            concat_axis=0,
+        ),
+        axis=0,
+    )
     child_columns = lax.dynamic_index_in_dim(everyone, col_id, axis=0, keepdims=False)
     schur_part = child_window.reshape(row_local * BLOCK_EXTENT, col_local * BLOCK_EXTENT) - jnp.dot(
         child_factor, child_columns.T, precision=highest

time: 830 us -> 895 us (1.078)
  starting transfers between devices: 6.99 us -> 82.9 us
  local copies, waits for them, and re-layouts: 109 us -> 91 us
  matrix products: 60.3 us -> 72.1 us
    all_gather x1 -> x0, waiting for transfers between devices: 89 us -> none  [per_device(): everyone = lax.all_gather(leading[None], 'row', axis=0, tiled=True)]
    all_to_all x0 -> x1, waiting for transfers between devices: none -> 86 us  [per_device(): lax.all_to_all(jnp.stack(lax.axis_size('row') * [array_here]), axis_name=...]
    all_to_all x1, starting transfers between devices: 6.87 us -> 74.8 us  [per_device(): lax.all_to_all(outgoing.reshape(-1, per_row * per_col, BLOCK_EXTENT, BLOC...]
    unnamed x24 -> x23, local copies, waits for them, and re-layouts: 28.3 us -> 6.96 us
    dot_general x1, matrix products: 20.5 us -> 32.4 us  [per_device(): jnp.dot(child_factor, child_columns.T, precision=highest)]
    another operation x24 -> x25, local copies, waits for them, and re-layouts: 16.3 us -> 25.8 us
    dynamic_slice x1 -> x0, local copies, waits for them, and re-layouts: 9.43 us -> none  [per_device(): lax.dynamic_index_in_dim(everyone, col_id, axis=0, keepdims=False)]
  transfers between devices with their start and end apart: 4 -> 4, of which waited for: 3 -> 3; matrix products, arithmetic and copies ran while one was open for 26% -> 25% of each run, Pallas kernels for 0% -> 0%
where the time goes in v1:
time: 895 us; the launch traced here: 885 us
  waiting for transfers between devices  310 us (35%)
  other arithmetic  308 us (34%)
  local copies, waits for them, and re-layouts  91 us (10%)
  starting transfers between devices  82.9 us (9%)
  matrix products  72.1 us (8%)
  between operations  20 us (2%)
    all_gather x1, waiting for transfers between devices, per_device(): lax.all_gather(solved.reshape(parent_row_blocks, sub_rows, panel_width),...  205 us
    all_to_all x1, waiting for transfers between devices, per_device(): lax.all_to_all(jnp.stack(lax.axis_size('row') * [array_here]), axis_name=...  86 us
    another operation x14, other arithmetic, per_device(): pivot_lower_factor = jnp.linalg.cholesky(parent_diag)  80.6 us
    another operation x14, other arithmetic, per_device(): child_low = jnp.linalg.cholesky(child_diag[0])  78.6 us
    all_to_all x1, starting transfers between devices, per_device(): lax.all_to_all(outgoing.reshape(-1, per_row * per_col, BLOCK_EXTENT, BLOC...  74.8 us
    scatter-add x1, other arithmetic, per_device(): assembled_front.at[target_rows, :, target_cols, :].add(arrived, mode='drop')  51.8 us
    another operation x2, other arithmetic, per_device(): jax.scipy.linalg.solve_triangular(pivot_lower_factor, own_rows.T, lower=T...  40.6 us
    another operation x3, other arithmetic, per_device(): jax.scipy.linalg.solve_triangular(child_low, child_rows.T, lower=True)  39.4 us
  transfers between devices with their start and end apart: 4, of which 3 were waited for; matrix products, arithmetic and copies ran while one was open for 25% of the time, Pallas kernels for 0%

profile of v1, /device:TPU:0, one launch (start us, length us, event | category | flops | bytes accessed | tf_op | source)
XLA Modules:
  0.0 884.8 jit_solution(13484040815482824368)
XLA Ops:
  13.2 11.7 %cholesky.286 = f32[128,128]{1,0:T(8,128)S(1)} custom-call(f32[128,128]{1,0:T(8,128)S(1)} %cholesky.426), custom_call_target="Cholesky" | custom-call | tf_op jit(solution)/shard_map/jit(cholesky)/cholesky | solution.py:56
  25.1 9.8 %custom-call.37 = f32[1,128,128]{1,2,0:T(8,128)S(1)} custom-call(f32[1,128,128]{2,1,0:T(8,128)S(1)} %get-tuple-element.91), custom_call_target="InvertDiagBlocksLowerTriangular" | custom-call | tf_op jit(solution)/shard_map/jit(cholesky)/cholesky | solution.py:56
  35.6 11.7 %cholesky.305 = f32[128,128]{1,0:T(8,128)S(1)} custom-call(f32[128,128]{1,0:T(8,128)S(1)} %cholesky.430), custom_call_target="Cholesky" | custom-call | tf_op jit(solution)/shard_map/jit(cholesky)/cholesky | solution.py:56
  47.3 10.0 %custom-call.38 = f32[1,128,128]{1,2,0:T(8,128)S(1)} custom-call(f32[1,128,128]{2,1,0:T(8,128)S(1)} %get-tuple-element.88), custom_call_target="InvertDiagBlocksLowerTriangular" | custom-call | tf_op jit(solution)/shard_map/jit(cholesky)/cholesky | solution.py:56
  57.9 11.7 %cholesky.326 = f32[128,128]{1,0:T(8,128)S(1)} custom-call(f32[128,128]{1,0:T(8,128)S(1)} %cholesky.435), custom_call_target="Cholesky" | custom-call | tf_op jit(solution)/shard_map/jit(cholesky)/cholesky | solution.py:56
  69.7 9.8 %custom-call.39 = f32[1,128,128]{1,2,0:T(8,128)S(1)} custom-call(f32[1,128,128]{2,1,0:T(8,128)S(1)} %get-tuple-element.85), custom_call_target="InvertDiagBlocksLowerTriangular" | custom-call | tf_op jit(solution)/shard_map/jit(cholesky)/cholesky | solution.py:56
  80.1 11.7 %cholesky.343 = f32[128,128]{1,0:T(8,128)S(1)} custom-call(f32[128,128]{1,0:T(8,128)S(1)} %convolution_subtract_fusion.10), custom_call_target="Cholesky" | custom-call | tf_op jit(solution)/shard_map/jit(cholesky)/cholesky | solution.py:56
  105.5 39.3 %custom-call.28 = f32[4,128,128]{1,2,0:T(8,128)S(1)} custom-call(f32[4,128,128]{2,1,0:T(8,128)S(1)} %get-tuple-element.11), custom_call_target="InvertDiagBlocksLowerTriangular" | custom-call | tf_op jit(solution)/shard_map/jit(_solve_triangular)/triangular_solve | solution.py:58
  189.0 11.7 %cholesky.358 = f32[128,128]{1,0:T(8,128)S(1)} custom-call(f32[128,128]{1,0:T(8,128)S(1)} %cholesky.439), custom_call_target="Cholesky" | custom-call | tf_op jit(solution)/shard_map/jit(cholesky)/cholesky | solution.py:42
  214.8 11.7 %cholesky.377 = f32[128,128]{1,0:T(8,128)S(1)} custom-call(f32[128,128]{1,0:T(8,128)S(1)} %cholesky.443), custom_call_target="Cholesky" | custom-call | tf_op jit(solution)/shard_map/jit(cholesky)/cholesky | solution.py:42
  227.2 10.2 %custom-call.41 = f32[1,128,128]{1,2,0:T(8,128)S(1)} custom-call(f32[1,128,128]{2,1,0:T(8,128)S(1)} %get-tuple-element.78), custom_call_target="InvertDiagBlocksLowerTriangular" | custom-call | tf_op jit(solution)/shard_map/jit(cholesky)/cholesky | solution.py:42
  239.7 11.7 %cholesky.398 = f32[128,128]{1,0:T(8,128)S(1)} custom-call(f32[128,128]{1,0:T(8,128)S(1)} %cholesky.448), custom_call_target="Cholesky" | custom-call | tf_op jit(solution)/shard_map/jit(cholesky)/cholesky | solution.py:42
  264.2 11.7 %cholesky.415 = f32[128,128]{1,0:T(8,128)S(1)} custom-call(f32[128,128]{1,0:T(8,128)S(1)} %convolution_subtract_fusion.9), custom_call_target="Cholesky" | custom-call | tf_op jit(solution)/shard_map/jit(cholesky)/cholesky | solution.py:42
  279.8 86.0 %all-to-all-done = f32[8,1,1024,512]{3,2,1,0:T(8,128)} async-done(((f32[8,1,1024,512]{3,2,1,0:T(8,128)}), f32[8,1,1024,512]{3,2,1,0:T(8,128)}, u32[]{:S(2)}, u32[]{:S(2)}) %all-to-all-start) | async-done | bytes 16777248 | tf_op jit(solution)/shard_map/all_to_all | solution.py:62
  365.9 32.4 %fusion = f32[256,8,8,128]{3,1,2,0:T(8,128)S(1)} fusion(f32[256,8,8,128]{3,2,1,0:T(8,128)} %bitcast.224, f32[128,2048]{1,0:T(8,128)} %copy-done.1, f32[128,2048]{1,0:T(8,128)S(1)} %fusion.56, f32[128,2048]{1,0:T(8,128)S(1)} %fusion.58, f32[128,2048]{1,0:T(8,128)S(1)} %fusion.16, f32[8,1,1024,512]{3,2,1,0:T(8,128)} %all-to-all-done, s32[]{:T(128)S(6)} %select_n.220), kind=kOutput, calls=%fused_computation.7 | convolution fusion | flops 12890144768 | bytes 23068676 | tf_op jit(solution)/shard_map/dot_general | solution.py:71
  405.0 16.0 %gather_fusion = f32[256,128,128]{2,1,0:T(8,128)} fusion(f32[16,128,8,128]{3,1,2,0:T(8,128)} %copy.73, s32[256]{0:T(256)S(1)} %reshape.580), kind=kCustom, calls=%fused_computation | custom fusion | bytes 33556480 | tf_op jit(solution)/shard_map/gather | solution.py:111
  421.0 11.4 %broadcast_select_fusion = f32[128,2,128,128]{3,2,1,0:T(8,128)} fusion(f32[128,2,128,128]{3,2,1,0:T(8,128)} %bitcast.216, pred[128,2]{1,0:T(8,128)(4,1)S(1)} %bitcast.233), kind=kLoop, calls=%fused_computation.8 | loop fusion | flops 4194304 | bytes 33554688 | tf_op jit(solution)/shard_map/select_n | solution.py:111
  432.4 74.8 %all-to-all-start.1 = ((f32[128,2,128,128]{3,2,1,0:T(8,128)}), f32[128,2,128,128]{3,2,1,0:T(8,128)}, u32[]{:S(2)}, u32[]{:S(2)}) async-start(f32[128,2,128,128]{3,2,1,0:T(8,128)} %broadcast_select_fusion), calls=%async_computation.1 | async-start | bytes 33554432 | tf_op jit(solution)/shard_map/all_to_all | solution.py:112
  518.3 39.3 %custom-call.29 = f32[4,128,128]{1,2,0:T(8,128)S(1)} custom-call(f32[4,128,128]{2,1,0:T(8,128)S(1)} %get-tuple-element.19), custom_call_target="InvertDiagBlocksLowerTriangular" | custom-call | tf_op jit(solution)/shard_map/jit(_solve_triangular)/triangular_solve | solution.py:44
  560.8 205.2 %all-gather.2.cloned.1.call-done = f32[24,128,512]{2,1,0:T(8,128)} async-done(((f32[24,8,512]{2,1,0:T(8,128)}), f32[24,128,512]{2,1,0:T(8,128)}) %all-gather.2.cloned.1.call-update) | async-done | bytes 6291472 | tf_op jit(solution)/shard_map/all_gather | solution.py:47
  773.5 51.8 %scatter_fusion = f32[24,128,4,128]{3,1,2,0:T(8,128)} fusion(f32[24,128,4,128]{3,1,2,0:T(8,128)} %broadcast_in_dim.106, s32[256]{0:T(256)S(1)} %reshape.588, f32[256,128,128]{2,1,0:T(8,128)} %bitcast.24), kind=kCustom, calls=%fused_computation.1 | custom fusion | flops 4194304 | bytes 50333696 | tf_op jit(solution)/shard_map/scatter-add | solution.py:122
  825.4 10.5 %copy.74 = f32[24,128,4,128]{3,2,1,0:T(4,128)} copy(f32[24,128,4,128]{3,1,2,0:T(8,128)} %scatter_fusion) | data formatting | bytes 12582912 | tf_op jit(solution)/shard_map/scatter-add | solution.py:122
  835.8 18.3 %all-reduce.3.cloned.1.call-done = f32[512,512]{1,0:T(8,128)} async-done(((f32[512,512]{1,0:T(8,128)}), f32[512,512]{1,0:T(8,128)}) %all-reduce.3.cloned.1.call-update) | async-done | bytes 1048592 | tf_op jit(solution)/shard_map/psum | solution.py:15
  854.1 16.1 %bitcast_subtract_fusion.1 = f32[3072,512]{1,0:T(8,128)} fusion(f32[384,8,4,128]{3,2,1,0:T(4,128)} %bitcast.218, f32[3072,512]{1,0:T(8,128)} %bitcast.223, f32[512,512]{1,0:T(8,128)} %all-reduce.3.cloned.1.call-done), kind=kOutput, calls=%fused_computation.9 | convolution fusion | flops 9665249280 | bytes 19922944 | tf_op jit(solution)/shard_map/dot_general | solution.py:126
  (171 shorter events, 146.6 us)
Async XLA Ops:
  7.2 5.5 copy-start.3
  105.5 45.1 %copy-start.4 = (f32[512,512]{1,0:T(8,128)}, f32[512,512]{1,0:T(8,128)S(1)}, u32[]{:S(2)}) copy-start(f32[512,512]{1,0:T(8,128)S(1)} %get-tuple-element.204) | copy-start | bytes 3145732
  144.8 5.7 copy-start
  156.9 1.0 copy-start.1
  172.2 8.5 copy-start.7
  172.2 11.2 %copy-start.8 = (s32[2]{0:T(128)S(1)}, s32[2]{0:T(128)}, u32[]{:S(2)}) copy-start(s32[2]{0:T(128)} %constant.261.clone.1) | copy-start | bytes 28
  172.2 193.7 %all-to-all-start = ((f32[8,1,1024,512]{3,2,1,0:T(8,128)}), f32[8,1,1024,512]{3,2,1,0:T(8,128)}, u32[]{:S(2)}, u32[]{:S(2)}) async-start(f32[8,1,1024,512]{3,2,1,0:T(8,128)} %stack.3), calls=%async_computation | async-start | bytes 33554432 | tf_op jit(solution)/shard_map/all_to_all | solution.py:62
  188.0 1.0 copy-start.5
  432.4 76.2 %copy-start.2 = (f32[512,512]{1,0:T(8,128)S(1)}, f32[512,512]{1,0:T(8,128)}, u32[]{:S(2)}) copy-start(f32[512,512]{1,0:T(8,128)} %get-tuple-element.73) | copy-start | bytes 3145732
  432.4 125.2 %copy-start.6 = (f32[24,1,1,1,8,512]{5,4,3,2,1,0:T(8,128)S(1)}, f32[24,1,1,1,8,512]{5,4,3,2,1,0:T(8,128)}, u32[]{:S(2)}) copy-start(f32[24,1,1,1,8,512]{5,4,3,2,1,0:T(8,128)} %param.11) | copy-start | bytes 1179652
  432.4 337.6 %all-to-all-start.1 = ((f32[128,2,128,128]{3,2,1,0:T(8,128)}), f32[128,2,128,128]{3,2,1,0:T(8,128)}, u32[]{:S(2)}, u32[]{:S(2)}) async-start(f32[128,2,128,128]{3,2,1,0:T(8,128)} %broadcast_select_fusion), calls=%async_computation.1 | async-start | bytes 33554432 | tf_op jit(solution)/shard_map/all_to_all | solution.py:112
  507.3 258.7 %all-gather.2.cloned.1.call-start = ((), (), s32[]{:S(2)}) async-start(), calls=%async_computation.2 | async-start | bytes 6684672 | tf_op jit(solution)/shard_map/all_gather | solution.py:47
  560.6 293.5 %all-reduce.3.cloned.1.call-start = ((), (), s32[]{:S(2)}) async-start(), calls=%async_computation.3 | async-start | bytes 2097152 | tf_op jit(solution)/shard_map/psum | solution.py:15
Sparse Core Ops, SparseCore 0:
  560.7 205.2 all-gather.1
  769.0 85.0 all-reduce.2
